TPU v7x, 32 devices: a whole 2x2x4 slice. The times are simulated.
32 devices in a mesh: parts: 2 (over y), tm: 4 (over x, core), cols: 4 (over z).
Axes of the slice: x: 2, y: 2, z: 4, core: 2. Of those that a mesh axis runs over, the one named last changes fastest.
Arguments:
- noise: float32 [16, 1024, 1024], P(('parts', 'tm'), None, 'cols'), parts along dimension 0, may hold values from -6 to 6
- inv_diag: float32 [16, 1024, 1024], P(('parts', 'tm'), None, 'cols'), parts along dimension 0, may hold values from -2 to 2, as said below
- coupling: float32 [16, 1024, 1024], P(('parts', 'tm'), None, 'cols'), parts along dimension 0, may hold values from -1 to 1, as said below
- order: int32 [1024], replicated, may hold values from 0 to 1023, each once
Outputs:
- sample: float32 [16, 1024, 1024], P(('parts', 'tm'), None, 'cols'), parts along dimension 0
There are 2 independent parts, one for each index of `parts`. A program takes and returns all parts, laid end to end along the dimension named above; an argument that names none is the same for every part. Nothing has to cross between parts.
Inputs may be any that keep to these rules, and one draw needn't show every extreme that they name: `order`: each of 0 to 1023 appears once. `inv_diag`: diagonal entries lie between 0.5 and 2, off-diagonal entries are small in magnitude. `coupling`: diagonal entries lie between 0.5 and 0.97, off-diagonal entries are small in magnitude.
All inputs are finite; a program needn't handle non-finite values.
Results may differ from a plain program's by a relative error of at most 0.00013.
Values sent between devices are 32-bit elements; how exact they have to be, the bound alone decides.
No kernel may reach another device: no remote copies, remote signals or barrier semaphores. Data moves between devices by JAX's collectives and lax.ppermute only.
A program may use at most 128 MiB of HBM per device.

v0:
```python
import jax
import jax.numpy as jnp
from jax import lax
from jax.sharding import PartitionSpec as P

low = jnp.bfloat16


def shifted(block, axis, distance):
    devices = range(lax.axis_size(axis))
    route = [(i - distance, i) for i in devices if i - distance in devices]
    return lax.ppermute(block, axis, route)


def split(value, count):
    parts = []
    rest = value
    for index in range(count):
        kept = lax.reduce_precision(rest, exponent_bits=8, mantissa_bits=7)
        parts.append(kept.astype(low))
        if index < count - 1:
            rest = rest - kept
    return parts


def bdot(left, right):
    return jnp.dot(left, right, preferred_element_type=jnp.float32)


def apply(matrix_parts, operand):
    high, small = matrix_parts
    operand_high, operand_small = split(operand, 2)
    return bdot(high, operand_high) + (bdot(high, operand_small) + bdot(small, operand_high))


def shards(noise, inv_diag, coupling, order):
    block_count = noise.shape[0]
    node_count = noise.shape[1]
    sample_count = noise.shape[2]
    pieces = 2 if sample_count % 256 == 0 else 1
    width = sample_count // pieces
    inv_full = lax.all_gather(inv_diag, "cols", axis=2, tiled=True)
    coupling_parts = [
        split(lax.all_gather(coupling[block], "cols", axis=1, tiled=True), 2)
        for block in range(block_count)
    ]
    driven = [apply(split(inv_full[block], 2), noise[block]) for block in range(block_count)]
    driven_pieces = [
        [driven[block][:, p * width : (p + 1) * width] for p in range(pieces)]
        for block in range(block_count)
    ]

    def chain(entering, piece, skip_last):
        carried = entering
        results = [None] * block_count
        for block in range(block_count - 1, -1, -1):
            if skip_last and block == block_count - 1:
                carried = driven_pieces[block][piece]
            else:
                carried = driven_pieces[block][piece] + apply(coupling_parts[block], carried)
            results[block] = carried
        return results

    first = [shifted(chain(None, p, True)[0], "tm", -1) for p in range(pieces)]

    def relay_step(step, entering):
        return [shifted(chain(entering[p], p, False)[0], "tm", -1) for p in range(pieces)]

    entering = lax.fori_loop(0, lax.axis_size("tm") - 2, relay_step, first)
    finals = [chain(entering[p], p, False) for p in range(pieces)]
    selector = (order[:, None] == jnp.arange(node_count, dtype=order.dtype)[None, :]).astype(low)
    outputs = []
    for block in range(block_count):
        field = jnp.concatenate([finals[p][block] for p in range(pieces)], axis=1)
        top, middle, bottom = split(field, 3)
        outputs.append(bdot(selector, top) + (bdot(selector, middle) + bdot(selector, bottom)))
    return jnp.stack(outputs, axis=0)


def solution(mesh):
    return jax.shard_map(
        shards,
        mesh=mesh,
        in_specs=(
            P(("parts", "tm"), None, "cols"),
            P(("parts", "tm"), None, "cols"),
            P(("parts", "tm"), None, "cols"),
            P(),
        ),
        out_specs=P(("parts", "tm"), None, "cols"),
        check_vma=False,
    )
```

profile of v0, /device:TPU:1, one launch (start us, length us, event | category | flops | bytes accessed | tf_op | source)
XLA Modules:
  0.0 439.5 jit_solution(6839977181822519246)
XLA Ops:
  6.5 3.0 fusion.150
  11.0 81.5 %all-gather.8.cloned.1.call-done = f32[1,1024,1024]{2,1,0:T(8,128)} async-done(((f32[1,1024,256]{2,1,0:T(8,128)}), f32[1,1024,1024]{2,1,0:T(8,128)}) %all-gather.8.cloned.1.call-update) | async-done | bytes 4194320 | tf_op jit(solution)/shard_map/all_gather | solution.py:44
  92.6 4.4 %reduce-precision_convert_fusion.13 = (bf16[1024,1024]{1,0:T(8,128)(2,1)S(1)}, bf16[1024,1024]{1,0:T(8,128)(2,1)}) fusion(f32[1,1024,1024]{2,1,0:T(8,128)} %all-gather.8.cloned.1.call-done), kind=kLoop, calls=%fused_computation.43 | loop fusion | flops 5242880 | bytes 8388608 | tf_op jit(solution)/shard_map/convert_element_type | solution.py:20
  97.0 76.5 %all-gather.10.cloned.1.call-done = f32[1,1024,1024]{2,1,0:T(8,128)} async-done(((f32[1,1024,256]{2,1,0:T(8,128)}), f32[1,1024,1024]{2,1,0:T(8,128)}) %all-gather.10.cloned.1.call-update) | async-done | bytes 4194320 | tf_op jit(solution)/shard_map/all_gather | solution.py:44
  173.5 5.0 %reduce-precision_convert_fusion.12 = (bf16[1024,1024]{1,0:T(8,128)(2,1)}, bf16[1024,1024]{1,0:T(8,128)(2,1)}) fusion(f32[1,1024,1024]{2,1,0:T(8,128)} %all-gather.10.cloned.1.call-done), kind=kLoop, calls=%fused_computation.41 | loop fusion | flops 5242880 | bytes 8388608 | tf_op jit(solution)/shard_map/convert_element_type | solution.py:20
  178.5 144.9 %all-gather.6.cloned.1.call-done = f32[2,1024,1024]{2,1,0:T(8,128)} async-done(((f32[2,1024,256]{2,1,0:T(8,128)}), f32[2,1024,1024]{2,1,0:T(8,128)}) %all-gather.6.cloned.1.call-update) | async-done | bytes 8388624 | tf_op jit(solution)/shard_map/all_gather | solution.py:42
  323.4 3.4 fusion.47
  326.9 3.8 fusion.97
  338.1 1.7 fusion.74
  339.8 1.7 fusion.71
  341.5 2.4 collective-permute-start.2
  343.8 2.1 collective-permute-start.3
  345.9 1.1 fusion.152
  347.0 2.0 copy.10
  349.0 2.0 copy.9
  351.1 2.3 fusion.151
  353.4 4.4 %collective-permute-done.3 = f32[1024,128]{0,1:T(8,128)S(1)} collective-permute-done((f32[1024,128]{0,1:T(8,128)}, f32[1024,128]{0,1:T(8,128)S(1)}, u32[]{:S(2)}, u32[]{:S(2)}) %collective-permute-start.3) | collective-permute-done | bytes 524320 | tf_op jit(solution)/shard_map/ppermute | solution.py:12
  357.8 54.2 %while.12 = (s32[]{:T(128)}, f32[1024,128]{0,1:T(8,128)S(1)}, f32[1024,128]{0,1:T(8,128)S(1)}, bf16[1024,1024]{1,0:T(8,128)(2,1)}, bf16[1024,1024]{1,0:T(8,128)(...) while((s32[]{:T(128)}, f32[1024,128]{0,1:T(8,128)S(1)}, ...), condition=%wide.region_1.0_spmd, body=%wide.region_0.0_spmd.sunk | while | flops 3226992640 | bytes 81789320 | solution.py:69
  357.8 2.5 fusion.228
  364.5 1.7 fusion.232
  366.2 1.9 collective-permute-start
  372.5 1.7 fusion.238
  374.2 1.9 collective-permute-start.1
  376.9 8.0 %collective-permute-done.1 = f32[1024,128]{0,1:T(8,128)S(1)} collective-permute-done((f32[1024,128]{0,1:T(8,128)}, f32[1024,128]{0,1:T(8,128)S(1)}, u32[]{:S(2)}, u32[]{:S(2)}) %collective-permute-start.1) | collective-permute-done | bytes 524320 | tf_op jit(solution)/shard_map/while/body/eval_jaxpr/ppermute | solution.py:12
  384.9 2.5 fusion.228
  391.7 1.7 fusion.232
  393.3 1.9 collective-permute-start
  399.7 1.7 fusion.238
  401.3 1.9 collective-permute-start.1
  404.0 8.0 %collective-permute-done.1 = f32[1024,128]{0,1:T(8,128)S(1)} collective-permute-done((f32[1024,128]{0,1:T(8,128)}, f32[1024,128]{0,1:T(8,128)S(1)}, u32[]{:S(2)}, u32[]{:S(2)}) %collective-permute-start.1) | collective-permute-done | bytes 524320 | tf_op jit(solution)/shard_map/while/body/eval_jaxpr/ppermute | solution.py:12
  412.0 2.6 fusion.136
  431.5 1.5 pad_maximum_fusion
  (102 shorter events, 44.3 us)
Async XLA Ops:
  6.5 86.0 %all-gather.8.cloned.1.call-start = ((), (), s32[]{:S(2)}) async-start(), calls=%async_computation.1 | async-start | bytes 5242880 | tf_op jit(solution)/shard_map/all_gather | solution.py:44
  9.6 163.9 %all-gather.10.cloned.1.call-start = ((), (), s32[]{:S(2)}) async-start(), calls=%async_computation.2 | async-start | bytes 5242880 | tf_op jit(solution)/shard_map/all_gather | solution.py:44
  10.3 313.1 %all-gather.6.cloned.1.call-start = ((), (), s32[]{:S(2)}) async-start(), calls=%async_computation | async-start | bytes 10485760 | tf_op jit(solution)/shard_map/all_gather | solution.py:42
  323.4 7.2 %copy-start.7 = (f32[2,1024,1024]{2,1,0:T(8,128)S(1)}, f32[2,1024,1024]{2,1,0:T(8,128)}, u32[]{:S(2)}) copy-start(f32[2,1024,1024]{2,1,0:T(8,128)} %all-gather.6.cloned.1.call-done) | copy-start | bytes 25165828
  326.8 4.0 copy-start.14
  330.8 1.6 copy-start.2
  331.6 14.3 %copy-start.8 = (f32[1024,256]{0,1:T(8,128)}, f32[1024,256]{0,1:T(8,128)S(1)}, u32[]{:S(2)}) copy-start(f32[1024,256]{0,1:T(8,128)S(1)} %fusion.69) | copy-start | bytes 3145732
  338.1 1.7 copy-start.15
  341.5 11.9 %collective-permute-start.2 = (f32[1024,128]{0,1:T(8,128)}, f32[1024,128]{0,1:T(8,128)S(1)}, u32[]{:S(2)}, u32[]{:S(2)}) collective-permute-start(f32[1024,128]{0,1:T(8,128)} %fusion.71), channel_id=1, source_target_pairs={{4,0},{8,4},{12,8},{5,1},{9,5},{13,9},{6,2},{10,6},{14,10},{7,3},{... | collective-permute-start | bytes 1572872 | tf_op jit(solution)/shard_map/ppermute | solution.py:12
  343.8 14.0 %collective-permute-start.3 = (f32[1024,128]{0,1:T(8,128)}, f32[1024,128]{0,1:T(8,128)S(1)}, u32[]{:S(2)}, u32[]{:S(2)}) collective-permute-start(f32[1024,128]{0,1:T(8,128)} %fusion.74), channel_id=1, source_target_pairs={{4,0},{8,4},{12,8},{5,1},{9,5},{13,9},{6,2},{10,6},{14,10},{7,3},{... | collective-permute-start | bytes 1572872 | tf_op jit(solution)/shard_map/ppermute | solution.py:12
  357.8 2.5 copy-start
  360.2 1.0 copy-start.11
  362.9 1.6 copy-start.3
  362.9 1.7 copy-start.13
  364.5 3.6 copy-start.5
  366.2 10.7 %collective-permute-start = (f32[1024,128]{0,1:T(8,128)}, f32[1024,128]{0,1:T(8,128)S(1)}, u32[]{:S(2)}, u32[]{:S(2)}) collective-permute-start(f32[1024,128]{0,1:T(8,128)} %fusion.232), channel_id=1, source_target_pairs={{4,0},{8,4},{12,8},{5,1},{9,5},{13,9},{6,2},{10,6},{14,10},{7,3},{... | collective-permute-start | bytes 1572872 | tf_op jit(solution)/shard_map/while/body/eval_jaxpr/ppermute | solution.py:12
  368.8 1.0 copy-start.10
  371.5 1.0 copy-start.12
  374.2 10.7 %collective-permute-start.1 = (f32[1024,128]{0,1:T(8,128)}, f32[1024,128]{0,1:T(8,128)S(1)}, u32[]{:S(2)}, u32[]{:S(2)}) collective-permute-start(f32[1024,128]{0,1:T(8,128)} %fusion.238), channel_id=1, source_target_pairs={{4,0},{8,4},{12,8},{5,1},{9,5},{13,9},{6,2},{10,6},{14,10},{7,3},{... | collective-permute-start | bytes 1572872 | tf_op jit(solution)/shard_map/while/body/eval_jaxpr/ppermute | solution.py:12
  384.9 2.5 copy-start
  387.4 1.0 copy-start.11
  390.0 1.6 copy-start.3
  390.0 1.7 copy-start.13
  391.6 3.6 copy-start.5
  393.3 10.7 %collective-permute-start = (f32[1024,128]{0,1:T(8,128)}, f32[1024,128]{0,1:T(8,128)S(1)}, u32[]{:S(2)}, u32[]{:S(2)}) collective-permute-start(f32[1024,128]{0,1:T(8,128)} %fusion.232), channel_id=1, source_target_pairs={{4,0},{8,4},{12,8},{5,1},{9,5},{13,9},{6,2},{10,6},{14,10},{7,3},{... | collective-permute-start | bytes 1572872 | tf_op jit(solution)/shard_map/while/body/eval_jaxpr/ppermute | solution.py:12
  398.6 1.0 copy-start.12
  401.3 10.7 %collective-permute-start.1 = (f32[1024,128]{0,1:T(8,128)}, f32[1024,128]{0,1:T(8,128)S(1)}, u32[]{:S(2)}, u32[]{:S(2)}) collective-permute-start(f32[1024,128]{0,1:T(8,128)} %fusion.238), channel_id=1, source_target_pairs={{4,0},{8,4},{12,8},{5,1},{9,5},{13,9},{6,2},{10,6},{14,10},{7,3},{... | collective-permute-start | bytes 1572872 | tf_op jit(solution)/shard_map/while/body/eval_jaxpr/ppermute | solution.py:12
  412.0 2.6 copy-start.6
  414.6 1.6 copy-start.1
  416.2 1.2 copy-start.9
  419.1 1.6 copy-start.4
  422.4 1.2 copy-start.16
  (2 other events, 1.9 us)
Sparse Core Ops, SparseCore 0:
  9.7 82.8 all-gather.7
  94.1 79.2 all-gather.9
  175.0 148.3 all-gather.5
where the time goes:
time: 440 us; the launch traced here: 439 us
  waiting for transfers between devices  326 us (74%)
  matrix products  59.5 us (14%)
  local copies, waits for them, and re-layouts  16.8 us (4%)
  between operations  13.4 us (3%)
  starting transfers between devices  12.2 us (3%)
  other arithmetic  10.9 us (2%)
    all_gather x2, waiting for transfers between devices, shards(): lax.all_gather(coupling[block], 'cols', axis=1, tiled=True)  158 us
    all_gather x1, waiting for transfers between devices, shards(): inv_full = lax.all_gather(inv_diag, 'cols', axis=2, tiled=True)  145 us
    dot_general x54, matrix products, bdot(): return jnp.dot(left, right, preferred_element_type=jnp.float32)  59.5 us
    ppermute x6, waiting for transfers between devices, shifted(): return lax.ppermute(block, axis, route)  22 us
    ppermute x6, starting transfers between devices, shifted(): return lax.ppermute(block, axis, route)  12.1 us
    convert_element_type x2, other arithmetic, split(): parts.append(kept.astype(low))  9.48 us
  transfers between devices with their start and end apart: 9, of which 8 were waited for; matrix products, arithmetic and copies ran while one was open for 6% of the time, Pallas kernels for 0%

commit v1 on v0

--- a/solution.py
+++ b/solution.py
@@ -4,6 +4,17 @@
 from jax.sharding import PartitionSpec as P
 
 low = jnp.bfloat16
+
+
+def gather_by_hops(value, axis, along):
+    size = lax.axis_size(axis)
+    right = [(i, (i + 1) % size) for i in range(size)]
+    shards = [value]
+    for far in range(1, size):
+        shards = [lax.ppermute(shards[0], axis, right), *shards]
+    out = jnp.concatenate(shards, axis=along)
+    turn = (lax.axis_index(axis) + 1) * shards[-1].shape[along]
+    return jnp.roll(out, turn, axis=along)
 
 
 def shifted(block, axis, distance):
@@ -39,7 +50,7 @@
     sample_count = noise.shape[2]
     pieces = 2 if sample_count % 256 == 0 else 1
     width = sample_count // pieces
-    inv_full = lax.all_gather(inv_diag, "cols", axis=2, tiled=True)
+    inv_full = gather_by_hops(inv_diag, "cols", 2)
     coupling_parts = [
         split(lax.all_gather(coupling[block], "cols", axis=1, tiled=True), 2)
         for block in range(block_count)

time: 440 us -> 413 us (0.939)
  the two profiles are of different devices: /device:TPU:1 before, /device:TPU:17 now
where the time goes in v1:
time: 413 us; the launch traced here: 412 us
  waiting for transfers between devices  277 us (67%)
  matrix products  54.9 us (13%)
  starting transfers between devices  28.3 us (7%)
  local copies, waits for them, and re-layouts  28.2 us (7%)
  between operations  13.9 us (3%)
  other arithmetic  9.94 us (2%)
    ppermute x3, waiting for transfers between devices, gather_by_hops(): shards = [lax.ppermute(shards[0], axis, right), *shards]  259 us
    dot_general x54, matrix products, bdot(): return jnp.dot(left, right, preferred_element_type=jnp.float32)  54.9 us
    ppermute x6, starting transfers between devices, shifted(): return lax.ppermute(block, axis, route)  24.6 us
    ppermute x6, waiting for transfers between devices, shifted(): return lax.ppermute(block, axis, route)  17.6 us
    unnamed x37, local copies, waits for them, and re-layouts  14 us
    convert_element_type x2, other arithmetic, split(): parts.append(kept.astype(low))  8.48 us
  transfers between devices with their start and end apart: 11, of which 7 were waited for; matrix products, arithmetic and copies ran while one was open for 11% of the time, Pallas kernels for 0%

profile of v1, /device:TPU:17, one launch (start us, length us, event | category | flops | bytes accessed | tf_op | source)
XLA Modules:
  0.0 412.2 jit_solution(7142200775461406472)
XLA Ops:
  6.5 3.1 fusion.150
  11.1 112.7 %collective-permute-done.2 = f32[2,1024,256]{2,1,0:T(8,128)S(1)} collective-permute-done((f32[2,1024,256]{2,1,0:T(8,128)S(1)}, f32[2,1024,256]{2,1,0:T(8,128)S(1)}, u32[]{:S(2)}, u32[]{:S(2)}) %collective-permute-start.2) | collective-permute-done | bytes 2097184 | tf_op jit(solution)/shard_map/ppermute | solution.py:14
  126.3 44.6 %collective-permute-done.3 = f32[2,1024,256]{2,1,0:T(8,128)} collective-permute-done((f32[2,1024,256]{2,1,0:T(8,128)S(1)}, f32[2,1024,256]{2,1,0:T(8,128)}, u32[]{:S(2)}, u32[]{:S(2)}) %collective-permute-start.3) | collective-permute-done | bytes 2097184 | tf_op jit(solution)/shard_map/ppermute | solution.py:14
  172.1 101.8 %collective-permute-done.4 = f32[2,1024,256]{2,1,0:T(8,128)} collective-permute-done((f32[2,1024,256]{2,1,0:T(8,128)}, f32[2,1024,256]{2,1,0:T(8,128)}, u32[]{:S(2)}, u32[]{:S(2)}) %collective-permute-start.4) | collective-permute-done | bytes 2097184 | tf_op jit(solution)/shard_map/ppermute | solution.py:14
  273.8 1.9 constant_dynamic-update-slice_fusion.7
  275.7 2.1 constant_dynamic-update-slice_fusion.6
  278.5 1.9 constant_dynamic-update-slice_fusion.3
  280.5 1.9 constant_dynamic-update-slice_fusion.2
  290.2 3.3 reduce-precision_convert_fusion.13
  295.6 1.6 fusion.70
  297.2 14.9 %collective-permute-start.6 = (f32[1024,128]{0,1:T(8,128)}, f32[1024,128]{0,1:T(8,128)S(1)}, u32[]{:S(2)}, u32[]{:S(2)}) collective-permute-start(f32[1024,128]{0,1:T(8,128)} %fusion.70), channel_id=1, source_target_pairs={{4,0},{8,4},{12,8},{5,1},{9,5},{13,9},{6,2},{10,6},{14,10},{7,3},{... | collective-permute-start | bytes 1572872 | tf_op jit(solution)/shard_map/ppermute | solution.py:23
  312.1 1.9 fusion.126
  314.9 1.6 fusion.67
  316.5 2.1 collective-permute-start.5
  319.6 2.1 copy.10
  321.7 2.0 copy.9
  323.8 5.2 %reduce-precision_convert_fusion.12 = (bf16[1024,1024]{1,0:T(8,128)(2,1)}, bf16[1024,1024]{1,0:T(8,128)(2,1)}) fusion(f32[1,1024,1024]{2,1,0:T(8,128)} %all-gather.7.cloned.1.call-done), kind=kLoop, calls=%fused_computation.41 | loop fusion | flops 5242880 | bytes 8388608 | tf_op jit(solution)/shard_map/convert_element_type | solution.py:31
  329.0 55.5 %while.12 = (s32[]{:T(128)}, f32[1024,128]{0,1:T(8,128)S(1)}, f32[1024,128]{0,1:T(8,128)S(1)}, bf16[1024,1024]{1,0:T(8,128)(2,1)}, bf16[1024,1024]{1,0:T(8,128)(...) while((s32[]{:T(128)}, f32[1024,128]{0,1:T(8,128)S(1)}, ...), condition=%wide.region_1.2_spmd, body=%wide.region_0.1_spmd.sunk | while | flops 3226992640 | bytes 81789320 | solution.py:80
  329.0 2.5 fusion.233
  336.4 1.7 fusion.238
  338.0 1.9 collective-permute-start.1
  344.4 1.6 fusion.232
  346.0 1.9 collective-permute-start
  348.7 8.0 %collective-permute-done = f32[1024,128]{0,1:T(8,128)S(1)} collective-permute-done((f32[1024,128]{0,1:T(8,128)}, f32[1024,128]{0,1:T(8,128)S(1)}, u32[]{:S(2)}, u32[]{:S(2)}) %collective-permute-start) | collective-permute-done | bytes 524320 | tf_op jit(solution)/shard_map/while/body/eval_jaxpr/ppermute | solution.py:23
  356.7 2.4 fusion.233
  364.1 1.7 fusion.238
  365.8 1.9 collective-permute-start.1
  372.1 1.6 fusion.232
  373.8 1.9 collective-permute-start
  376.5 8.0 %collective-permute-done = f32[1024,128]{0,1:T(8,128)S(1)} collective-permute-done((f32[1024,128]{0,1:T(8,128)}, f32[1024,128]{0,1:T(8,128)S(1)}, u32[]{:S(2)}, u32[]{:S(2)}) %collective-permute-start) | collective-permute-done | bytes 524320 | tf_op jit(solution)/shard_map/while/body/eval_jaxpr/ppermute | solution.py:23
  384.5 2.6 fusion.128
  404.0 1.5 pad_maximum_fusion
  (121 shorter events, 54.2 us)
Async XLA Ops:
  6.5 3.2 copy-start.18
  6.5 283.6 %all-gather.5.cloned.1.call-start = ((), (), s32[]{:S(2)}) async-start(), calls=%async_computation | async-start | bytes 5242880 | tf_op jit(solution)/shard_map/all_gather | solution.py:55
  9.7 314.1 %all-gather.7.cloned.1.call-start = ((), (), s32[]{:S(2)}) async-start(), calls=%async_computation.1 | async-start | bytes 5242880 | tf_op jit(solution)/shard_map/all_gather | solution.py:55
  9.7 114.1 %collective-permute-start.2 = (f32[2,1024,256]{2,1,0:T(8,128)S(1)}, f32[2,1024,256]{2,1,0:T(8,128)S(1)}, u32[]{:S(2)}, u32[]{:S(2)}) collective-permute-start(f32[2,1024,256]{2,1,0:T(8,128)S(1)} %copy-done.18), channel_id=1, source_target_pairs={{0,1},{1,2},{2,3},{3,0},{4,5},{5,6},{6,7},{7,4},{8,9},{9,10},{10,1... | collective-permute-start | bytes 6291464 | tf_op jit(solution)/shard_map/ppermute | solution.py:14
  123.8 1.3 copy-start.19
  125.1 45.8 %collective-permute-start.3 = (f32[2,1024,256]{2,1,0:T(8,128)S(1)}, f32[2,1024,256]{2,1,0:T(8,128)}, u32[]{:S(2)}, u32[]{:S(2)}) collective-permute-start(f32[2,1024,256]{2,1,0:T(8,128)S(1)} %collective-permute-done.2), channel_id=1, source_target_pairs={{0,1},{1,2},{2,3},{3,0},{4,5},{5,6},{6,7},{7,4},{8,9},{9,10},{10,1... | collective-permute-start | bytes 6291464 | tf_op jit(solution)/shard_map/ppermute | solution.py:14
  170.9 102.9 %collective-permute-start.4 = (f32[2,1024,256]{2,1,0:T(8,128)}, f32[2,1024,256]{2,1,0:T(8,128)}, u32[]{:S(2)}, u32[]{:S(2)}) collective-permute-start(f32[2,1024,256]{2,1,0:T(8,128)} %collective-permute-done.3), channel_id=1, source_target_pairs={{0,1},{1,2},{2,3},{3,0},{4,5},{5,6},{6,7},{7,4},{8,9},{9,10},{10,1... | collective-permute-start | bytes 6291464 | tf_op jit(solution)/shard_map/ppermute | solution.py:14
  275.7 2.2 copy-start.20
  282.7 1.6 copy-start.14
  286.6 2.0 copy-start.15
  290.1 5.0 %copy-start.7 = (f32[1024,256]{0,1:T(8,128)}, f32[1024,256]{0,1:T(8,128)S(1)}, u32[]{:S(2)}) copy-start(f32[1024,256]{0,1:T(8,128)S(1)} %convolution_add_fusion.3) | copy-start | bytes 3145732
  293.5 18.7 %copy-start.2 = (bf16[1024,1024]{1,0:T(8,128)(2,1)}, bf16[1024,1024]{1,0:T(8,128)(2,1)S(1)}, u32[]{:S(2)}) copy-start(bf16[1024,1024]{1,0:T(8,128)(2,1)S(1)} %get-tuple-element.182) | copy-start | bytes 6291460
  297.2 16.8 %copy-start.8 = (f32[1024,256]{0,1:T(8,128)S(1)}, f32[1024,256]{0,1:T(8,128)}, u32[]{:S(2)}) copy-start(f32[1024,256]{0,1:T(8,128)} %copy-done.7) | copy-start | bytes 3145732
  297.2 31.8 %collective-permute-start.6 = (f32[1024,128]{0,1:T(8,128)}, f32[1024,128]{0,1:T(8,128)S(1)}, u32[]{:S(2)}, u32[]{:S(2)}) collective-permute-start(f32[1024,128]{0,1:T(8,128)} %fusion.70), channel_id=1, source_target_pairs={{4,0},{8,4},{12,8},{5,1},{9,5},{13,9},{6,2},{10,6},{14,10},{7,3},{... | collective-permute-start | bytes 1572872 | tf_op jit(solution)/shard_map/ppermute | solution.py:23
  316.5 12.5 %collective-permute-start.5 = (f32[1024,128]{0,1:T(8,128)}, f32[1024,128]{0,1:T(8,128)S(1)}, u32[]{:S(2)}, u32[]{:S(2)}) collective-permute-start(f32[1024,128]{0,1:T(8,128)} %fusion.67), channel_id=1, source_target_pairs={{4,0},{8,4},{12,8},{5,1},{9,5},{13,9},{6,2},{10,6},{14,10},{7,3},{... | collective-permute-start | bytes 1572872 | tf_op jit(solution)/shard_map/ppermute | solution.py:23
  329.0 2.5 copy-start.5
  331.4 1.6 copy-start
  331.5 1.7 copy-start.10
  334.7 1.6 copy-start.3
  334.7 1.7 copy-start.12
  338.0 10.7 %collective-permute-start.1 = (f32[1024,128]{0,1:T(8,128)}, f32[1024,128]{0,1:T(8,128)S(1)}, u32[]{:S(2)}, u32[]{:S(2)}) collective-permute-start(f32[1024,128]{0,1:T(8,128)} %fusion.238), channel_id=1, source_target_pairs={{4,0},{8,4},{12,8},{5,1},{9,5},{13,9},{6,2},{10,6},{14,10},{7,3},{... | collective-permute-start | bytes 1572872 | tf_op jit(solution)/shard_map/while/body/eval_jaxpr/ppermute | solution.py:23
  346.0 10.7 %collective-permute-start = (f32[1024,128]{0,1:T(8,128)}, f32[1024,128]{0,1:T(8,128)S(1)}, u32[]{:S(2)}, u32[]{:S(2)}) collective-permute-start(f32[1024,128]{0,1:T(8,128)} %fusion.232), channel_id=1, source_target_pairs={{4,0},{8,4},{12,8},{5,1},{9,5},{13,9},{6,2},{10,6},{14,10},{7,3},{... | collective-permute-start | bytes 1572872 | tf_op jit(solution)/shard_map/while/body/eval_jaxpr/ppermute | solution.py:23
  356.7 2.5 copy-start.5
  359.2 1.6 copy-start
  359.2 1.7 copy-start.10
  362.4 1.6 copy-start.3
  362.4 1.7 copy-start.12
  365.8 10.7 %collective-permute-start.1 = (f32[1024,128]{0,1:T(8,128)}, f32[1024,128]{0,1:T(8,128)S(1)}, u32[]{:S(2)}, u32[]{:S(2)}) collective-permute-start(f32[1024,128]{0,1:T(8,128)} %fusion.238), channel_id=1, source_target_pairs={{4,0},{8,4},{12,8},{5,1},{9,5},{13,9},{6,2},{10,6},{14,10},{7,3},{... | collective-permute-start | bytes 1572872 | tf_op jit(solution)/shard_map/while/body/eval_jaxpr/ppermute | solution.py:23
  373.8 10.7 %collective-permute-start = (f32[1024,128]{0,1:T(8,128)}, f32[1024,128]{0,1:T(8,128)S(1)}, u32[]{:S(2)}, u32[]{:S(2)}) collective-permute-start(f32[1024,128]{0,1:T(8,128)} %fusion.232), channel_id=1, source_target_pairs={{4,0},{8,4},{12,8},{5,1},{9,5},{13,9},{6,2},{10,6},{14,10},{7,3},{... | collective-permute-start | bytes 1572872 | tf_op jit(solution)/shard_map/while/body/eval_jaxpr/ppermute | solution.py:23
  384.5 2.6 copy-start.1
  388.3 1.6 copy-start.4
  391.9 1.6 copy-start.6
  (8 other events, 8.7 us)
Sparse Core Ops, SparseCore 0:
  9.8 115.4 all-gather.4
  172.2 116.3 all-gather.6
